TPU v7x, 512 devices: a whole 4x4x16 slice. The times are simulated.
512 devices in a mesh: gx: 64 (over z, y), gy: 8 (over x, core).
Axes of the slice: x: 4, y: 4, z: 16, core: 2. Of those that a mesh axis runs over, the one named last changes fastest.
Arguments:
- rhs: float32 [64, 8, 128, 128], P('gx', 'gy'), may hold values from -57 to 57
- face_rows: int32 [64, 8, 4, 128], P('gx', 'gy'), may hold values from 0 to 127
- margin_weight: float32 [64, 8, 4, 128], P('gx', 'gy'), may hold values from 0.2 to 1
- local_blocks: bfloat16 [64, 8, 1, 128, 128], P('gx', 'gy'), may hold values from -0.4 to 4.4
- subdomain_inverse: bfloat16 [64, 8, 128, 640], P('gx', 'gy'), may hold values from -0.4 to 1.8
- coarse_basis: bfloat16 [64, 8, 128, 32], P('gx', 'gy'), may hold values from -0.5 to 0.5
- coarse_inverse: bfloat16 [64, 8, 32, 16384], P('gx', 'gy'), may hold values from -0.09765625 to 0.09765625
- coarse_map: int32 [512], replicated, may hold values from 0 to 511, each once
Outputs:
- solution: float32 [64, 8, 128, 128], P('gx', 'gy')
- relative_residual: float32 [128], replicated
Inputs may be any that keep to these rules, and one draw needn't show every extreme that they name: `face_rows`: rows of the subdomain, repeats possible. `coarse_map`: every position once.
All inputs are finite; a program needn't handle non-finite values.
Results may differ from a plain program's by a relative error of at most 0.004.
Values may be sent and summed in bfloat16 or wider, within the bound.
No kernel may reach another device: no remote copies, remote signals or barrier semaphores. Data moves between devices by JAX's collectives and lax.ppermute only.
A program may use at most 64 MiB of HBM per device.

v0:
```python
import jax
import numpy as np
import jax.numpy as jnp
from jax import lax
from jax.sharding import PartitionSpec as P

EPSILON = 1e-06
KEPT_SHARE = 1.0 / 64


def neighbours(rows, axis):
    count = lax.axis_size(axis)
    up = [(i, i + 1) for i in range(count - 1)]
    down = [(i + 1, i) for i in range(count - 1)]
    return (lax.ppermute(rows[1], axis, up), lax.ppermute(rows[0], axis, down))


def exchange(packs):
    below_first, above_first = neighbours(packs[0:2], "gx")
    below_second, above_second = neighbours(packs[2:4], "gy")
    return jnp.stack([below_first, above_first, below_second, above_second], axis=0)


def allsum(value):
    value = lax.psum(value, "gy")
    for axis in ("gx",):
        count = lax.axis_size(axis)
        if count & count - 1:
            value = lax.psum(value, axis)
            continue
        step = 1
        while step < count:
            value = value + lax.ppermute(value, axis, [(i, i ^ step) for i in range(count)])
            step *= 2
    return value


GATHER_ROUNDS = (("gx", 32), ("gx", 16), ("gx", 8), ("gx", 4), ("gx", 2), ("gx", 1))


def gather_rounds(count_x, count_y):
    sizes = {"gx": count_x, "gy": count_y}
    return tuple(((axis, step) for axis, step in GATHER_ROUNDS if step < sizes[axis]))


def doubling_gather(block, rounds):
    held = block[None]
    for axis, step in rounds:
        count = lax.axis_size(axis)
        got = lax.ppermute(held, axis, [(i, i ^ step) for i in range(count)])
        upper = lax.axis_index(axis) // step % 2 == 1
        held = jnp.where(
            upper, jnp.concatenate([got, held], axis=0), jnp.concatenate([held, got], axis=0)
        )
    return lax.all_gather(held.reshape(-1, block.shape[-1]), "gy", axis=0, tiled=True)


def gathered_order(rounds, count_y):
    order = []
    for outer in range(count_y):
        for position in range(2 ** len(rounds)):
            index = {"gx": 0, "gy": outer}
            for bit, (axis, step) in enumerate(rounds):
                index[axis] += (position >> bit & 1) * step
            order.append(index["gx"] * count_y + index["gy"])
    return np.asarray(order, np.int32)


def least_squares(scale_norm, first_dot, first_norm, cross_dot, second_dot, second_norm):
    radius_one = jnp.sqrt(first_dot * first_dot + first_norm * first_norm)
    cosine_one = first_dot / radius_one
    sine_one = first_norm / radius_one
    upper_entry = cosine_one * cross_dot + sine_one * second_dot
    lower_entry = cosine_one * second_dot - sine_one * cross_dot
    radius_two = jnp.sqrt(lower_entry * lower_entry + second_norm * second_norm)
    cosine_two = lower_entry / radius_two
    sine_two = second_norm / radius_two
    weight_two = -cosine_two * sine_one * scale_norm / radius_two
    weight_one = (cosine_one * scale_norm - upper_entry * weight_two) / radius_one
    return (weight_one, weight_two, sine_one * sine_two)


def on_device(
    rhs,
    face_rows,
    margin_weight,
    local_blocks,
    subdomain_inverse,
    coarse_basis,
    coarse_inverse,
    coarse_map,
):
    right_side = rhs[0, 0]
    margin_rows = face_rows[0, 0]
    margin_weights = margin_weight[0, 0]
    local_block = local_blocks[0, 0]
    inverse_rows = subdomain_inverse[0, 0]
    basis = coarse_basis[0, 0]
    coarse_rows = coarse_inverse[0, 0]
    owned_rows = right_side.shape[0]
    system_count = right_side.shape[1]
    basis_count = basis.shape[1]
    block_rows = local_block.shape[1]
    count_x = lax.axis_size("gx")
    count_y = lax.axis_size("gy")
    rounds = gather_rounds(count_x, count_y)
    gathered_map = coarse_map[gathered_order(rounds, count_y)]
    selection = (
        gathered_map[:, None] == jnp.arange(gathered_map.shape[0], dtype=jnp.int32)[None, :]
    ).astype(jnp.bfloat16)

    def margin_of(field):
        return exchange(field[margin_rows])

    def coarse_gather(residual):
        return doubling_gather(residual, rounds)

    def precondition(rounded, margin):
        extended = jnp.concatenate([rounded, margin.reshape(-1, system_count)], axis=0)
        local_part = jnp.dot(inverse_rows, extended, preferred_element_type=jnp.float32)
        residual = lax.dot_general(
            basis, rounded, (((0,), (0,)), ((), ())), preferred_element_type=jnp.float32
        ).astype(jnp.bfloat16)
        gathered = coarse_gather(residual).reshape(selection.shape[0], -1)
        placed = lax.dot_general(
            selection, gathered, (((0,), (0,)), ((), ())), preferred_element_type=jnp.float32
        ).astype(jnp.bfloat16)
        solved = jnp.dot(
            coarse_rows, placed.reshape(-1, system_count), preferred_element_type=jnp.float32
        )
        return local_part + jnp.dot(
            basis, solved.astype(jnp.bfloat16), preferred_element_type=jnp.float32
        )

    def apply_operator(vector):
        rounded = vector.astype(jnp.bfloat16)
        own_part = jnp.einsum(
            "brc,bcn->brn",
            local_block,
            rounded.reshape(-1, block_rows, system_count),
            preferred_element_type=jnp.float32,
        ).reshape(owned_rows, system_count)
        weighted = margin_weights[:, :, None] * margin_of(rounded).astype(jnp.float32)
        coupling = (
            jnp.zeros((owned_rows, system_count), jnp.float32)
            .at[margin_rows.reshape(-1)]
            .add(weighted.reshape(-1, system_count))
        )
        return own_part - coupling

    def column_norm(vector):
        return jnp.sqrt(allsum(jnp.sum(vector * vector, axis=0)) + EPSILON)

    def guarded_norm(expanded, whole, remainder):
        kept = jnp.all(jnp.isfinite(expanded) & (expanded >= KEPT_SHARE * whole))
        return lax.cond(kept, lambda vector: jnp.sqrt(expanded + EPSILON), column_norm, remainder)

    rhs_margin = margin_of(right_side)
    scale_norm = column_norm(right_side)
    krylov_one = right_side / scale_norm
    margin_one = rhs_margin / scale_norm
    precond_one = precondition(krylov_one.astype(jnp.bfloat16), margin_one.astype(jnp.bfloat16))
    applied = apply_operator(precond_one)
    applied_margin = margin_of(applied)
    sums = allsum(
        jnp.stack(
            [
                jnp.sum(applied * krylov_one, axis=0),
                jnp.sum(applied * applied, axis=0),
                jnp.sum(krylov_one * krylov_one, axis=0),
            ]
        )
    )
    first_dot = sums[0]
    remainder = applied - first_dot * krylov_one
    expanded = sums[1] - 2.0 * first_dot * first_dot + first_dot * first_dot * sums[2]
    first_norm = guarded_norm(expanded, sums[1], remainder)
    krylov_two = remainder / first_norm
    margin_two = (applied_margin - first_dot * margin_one) / first_norm
    precond_two = precondition(krylov_two.astype(jnp.bfloat16), margin_two.astype(jnp.bfloat16))
    applied = apply_operator(precond_two)
    dots = allsum(
        jnp.stack(
            [
                jnp.sum(applied * krylov_one, axis=0),
                jnp.sum(applied * krylov_two, axis=0),
                jnp.sum(applied * applied, axis=0),
                jnp.sum(krylov_one * krylov_one, axis=0),
                jnp.sum(krylov_one * krylov_two, axis=0),
                jnp.sum(krylov_two * krylov_two, axis=0),
            ]
        )
    )
    cross_dot = dots[0]
    second_dot = dots[1]
    remainder = applied - cross_dot * krylov_one - second_dot * krylov_two
    expanded = (
        dots[2]
        - 2.0 * cross_dot * cross_dot
        - 2.0 * second_dot * second_dot
        + cross_dot * cross_dot * dots[3]
        + 2.0 * cross_dot * second_dot * dots[4]
        + second_dot * second_dot * dots[5]
    )
    second_norm = guarded_norm(expanded, dots[2], remainder)
    weight_one, weight_two, relative = least_squares(
        scale_norm, first_dot, first_norm, cross_dot, second_dot, second_norm
    )
    solution = weight_one * precond_one + weight_two * precond_two
    return (solution[None, None], relative)


def solution(mesh):
    return jax.shard_map(
        on_device,
        mesh=mesh,
        in_specs=(
            P("gx", "gy", None, None),
            P("gx", "gy", None, None),
            P("gx", "gy", None, None),
            P("gx", "gy", None, None, None),
            P("gx", "gy", None, None),
            P("gx", "gy", None, None),
            P("gx", "gy", None, None),
            P(),
        ),
        out_specs=(P("gx", "gy", None, None), P()),
        check_vma=False,
    )
```

profile of v0, /device:TPU:8, one launch (start us, length us, event | category | flops | bytes accessed | tf_op | source)
XLA Modules:
  0.0 481.7 jit_solution(6558370175424277475)
XLA Ops:
  8.2 14.6 %psum.35 = f32[128]{0:T(128)S(1)} all-reduce(f32[128]{0:T(128)S(1)} %multiply_reduce_fusion.10), channel_id=1, replica_groups=mesh['gx'=64,'gy'=8] {'gy'}, use_global_device_ids=true, to_apply=%region_1.0 | all-reduce | flops 128 | bytes 1024 | tf_op jit(solution)/shard_map/psum | solution.py:25
  22.8 5.5 %collective-permute-start.12 = (f32[128]{0:T(128)S(1)}, f32[128]{0:T(128)S(1)}, u32[]{:S(2)}, u32[]{:S(2)}) collective-permute-start(f32[128]{0:T(128)S(1)} %psum.35), channel_id=1, source_target_pairs={{0,8},{8,0},{16,24},{24,16},{32,40},{40,32},{48,56},{56,48},{64,72... | collective-permute-start | bytes 1544 | tf_op jit(solution)/shard_map/ppermute | solution.py:33
  32.5 4.3 collective-permute-done.13
  48.6 7.9 %collective-permute-start.16 = (f32[128]{0:T(128)S(1)}, f32[128]{0:T(128)S(1)}, u32[]{:S(2)}, u32[]{:S(2)}) collective-permute-start(f32[128]{0:T(128)S(1)} %add.222), channel_id=1, source_target_pairs={{0,128},{8,136},{16,144},{24,152},{32,160},{40,168},{48,176},{56,1... | collective-permute-start | bytes 1544 | tf_op jit(solution)/shard_map/ppermute | solution.py:33
  58.0 14.1 %collective-permute-start.17 = (f32[128]{0:T(128)S(1)}, f32[128]{0:T(128)S(1)}, u32[]{:S(2)}, u32[]{:S(2)}) collective-permute-start(f32[128]{0:T(128)S(1)} %add.223), channel_id=1, source_target_pairs={{0,256},{8,264},{16,272},{24,280},{32,288},{40,296},{48,304},{56,3... | collective-permute-start | bytes 1544 | tf_op jit(solution)/shard_map/ppermute | solution.py:33
  74.6 12.6 %collective-permute-start.22 = (bf16[1,32,128]{2,1,0:T(8,128)(2,1)S(1)}, bf16[1,32,128]{2,1,0:T(8,128)(2,1)S(1)}, u32[]{:S(2)}, u32[]{:S(2)}) collective-permute-start(bf16[1,32,128]{2,1,0:T(8,128)(2,1)S(1)} %fusion.2), channel_id=1, source_target_pairs={{0,256},{8,264},{16,272},{24,280},{32,288},{40,296},{48,304},{56,3... | collective-permute-start | bytes 24584 | tf_op jit(solution)/shard_map/ppermute | solution.py:50
  88.9 6.4 %collective-permute-start.23 = (bf16[2,32,128]{2,1,0:T(8,128)(2,1)S(1)}, bf16[2,32,128]{2,1,0:T(8,128)(2,1)S(1)}, u32[]{:S(2)}, u32[]{:S(2)}) collective-permute-start(bf16[2,32,128]{2,1,0:T(8,128)(2,1)S(1)} %maximum_select_fusion.10), channel_id=1, source_target_pairs={{0,128},{8,136},{16,144},{24,152},{32,160},{40,168},{48,176},{56,1... | collective-permute-start | bytes 49160 | tf_op jit(solution)/shard_map/ppermute | solution.py:50
  111.4 4.3 collective-permute-start.26
  115.7 4.1 collective-permute-done.26
  122.3 5.8 %collective-permute-done.27 = bf16[32,32,128]{2,1,0:T(8,128)(2,1)S(1)} collective-permute-done((bf16[32,32,128]{2,1,0:T(8,128)(2,1)S(1)}, bf16[32,32,128]{2,1,0:T(8,128)(2,1)S(1)}, u32[]{:S(2)}, u32[]{:S(2)}) %collective-permute-start.27) | collective-permute-done | bytes 262176 | tf_op jit(solution)/shard_map/ppermute | solution.py:50
  143.3 24.8 %all-gather.3.cloned.1.call-done = bf16[16384,128]{1,0:T(8,128)(2,1)} async-done(((bf16[2048,128]{1,0:T(8,128)(2,1)}), bf16[16384,128]{1,0:T(8,128)(2,1)}) %all-gather.3.cloned.1.call-update) | async-done | bytes 4194320 | tf_op jit(solution)/shard_map/all_gather | solution.py:55
  168.1 7.4 %reshape.132 = bf16[512,4096]{1,0:T(8,128)(2,1)} reshape(bf16[16384,128]{1,0:T(8,128)(2,1)} %all-gather.3.cloned.1.call-done) | data formatting | bytes 8388608 | tf_op jit(solution)/shard_map/reshape | solution.py:124
  175.4 6.6 %convolution_convert_fusion.1 = bf16[512,4096]{1,0:T(8,128)(2,1)} fusion(bf16[512,4096]{1,0:T(8,128)(2,1)} %reshape.132, s32[512]{0:T(512)S(1)} %gather_fusion.1), kind=kOutput, calls=%fused_computation.10 | convolution fusion | flops 2149842944 | bytes 8390656 | tf_op jit(solution)/shard_map/dot_general | solution.py:125
  182.0 7.5 %reshape.133 = bf16[16384,128]{1,0:T(8,128)(2,1)} reshape(bf16[512,4096]{1,0:T(8,128)(2,1)} %convolution_convert_fusion.1) | data formatting | bytes 8388608 | tf_op jit(solution)/shard_map/reshape | solution.py:129
  208.4 14.6 %psum.36 = f32[3,128]{1,0:T(4,128)S(1)} all-reduce(f32[3,128]{1,0:T(4,128)S(1)} %pad_maximum_fusion.4), channel_id=1, replica_groups=mesh['gx'=64,'gy'=8] {'gy'}, use_global_device_ids=true, to_apply=%region_6.7 | all-reduce | flops 384 | bytes 3072 | tf_op jit(solution)/shard_map/psum | solution.py:25
  235.4 4.1 collective-permute-start.34
  241.1 4.9 %collective-permute-start.35 = (f32[3,128]{1,0:T(4,128)S(1)}, f32[3,128]{1,0:T(4,128)S(1)}, u32[]{:S(2)}, u32[]{:S(2)}) collective-permute-start(f32[3,128]{1,0:T(4,128)S(1)} %add.239), channel_id=1, source_target_pairs={{0,64},{8,72},{16,80},{24,88},{32,96},{40,104},{48,112},{56,120},{... | collective-permute-start | bytes 4616 | tf_op jit(solution)/shard_map/ppermute | solution.py:33
  247.6 9.2 %collective-permute-start.36 = (f32[3,128]{1,0:T(4,128)S(1)}, f32[3,128]{1,0:T(4,128)S(1)}, u32[]{:S(2)}, u32[]{:S(2)}) collective-permute-start(f32[3,128]{1,0:T(4,128)S(1)} %add.240), channel_id=1, source_target_pairs={{0,128},{8,136},{16,144},{24,152},{32,160},{40,168},{48,176},{56,1... | collective-permute-start | bytes 4616 | tf_op jit(solution)/shard_map/ppermute | solution.py:33
  258.3 13.0 %collective-permute-start.37 = (f32[3,128]{1,0:T(4,128)S(1)}, f32[3,128]{1,0:T(4,128)S(1)}, u32[]{:S(2)}, u32[]{:S(2)}) collective-permute-start(f32[3,128]{1,0:T(4,128)S(1)} %add.241), channel_id=1, source_target_pairs={{0,256},{8,264},{16,272},{24,280},{32,288},{40,296},{48,304},{56,3... | collective-permute-start | bytes 4616 | tf_op jit(solution)/shard_map/ppermute | solution.py:33
  274.4 12.6 %collective-permute-start.42 = (bf16[1,32,128]{2,1,0:T(8,128)(2,1)S(1)}, bf16[1,32,128]{2,1,0:T(8,128)(2,1)S(1)}, u32[]{:S(2)}, u32[]{:S(2)}) collective-permute-start(bf16[1,32,128]{2,1,0:T(8,128)(2,1)S(1)} %fusion.3), channel_id=1, source_target_pairs={{0,256},{8,264},{16,272},{24,280},{32,288},{40,296},{48,304},{56,3... | collective-permute-start | bytes 24584 | tf_op jit(solution)/shard_map/ppermute | solution.py:50
  288.6 7.5 %collective-permute-start.43 = (bf16[2,32,128]{2,1,0:T(8,128)(2,1)S(1)}, bf16[2,32,128]{2,1,0:T(8,128)(2,1)S(1)}, u32[]{:S(2)}, u32[]{:S(2)}) collective-permute-start(bf16[2,32,128]{2,1,0:T(8,128)(2,1)S(1)} %maximum_select_fusion.11), channel_id=1, source_target_pairs={{0,128},{8,136},{16,144},{24,152},{32,160},{40,168},{48,176},{56,1... | collective-permute-start | bytes 49160 | tf_op jit(solution)/shard_map/ppermute | solution.py:50
  314.7 4.7 collective-permute-done.46
  323.4 4.3 collective-permute-done.47
  340.4 26.8 %all-gather.5.cloned.1.call-done = bf16[16384,128]{1,0:T(8,128)(2,1)} async-done(((bf16[2048,128]{1,0:T(8,128)(2,1)}), bf16[16384,128]{1,0:T(8,128)(2,1)}) %all-gather.5.cloned.1.call-update) | async-done | bytes 4194320 | tf_op jit(solution)/shard_map/all_gather | solution.py:55
  367.2 7.4 %reshape.135 = bf16[512,4096]{1,0:T(8,128)(2,1)} reshape(bf16[16384,128]{1,0:T(8,128)(2,1)} %all-gather.5.cloned.1.call-done) | data formatting | bytes 8388608 | tf_op jit(solution)/shard_map/reshape | solution.py:124
  374.6 6.6 %convolution_convert_fusion = bf16[512,4096]{1,0:T(8,128)(2,1)} fusion(bf16[512,4096]{1,0:T(8,128)(2,1)} %reshape.135, s32[512]{0:T(512)S(1)} %gather_fusion.1), kind=kOutput, calls=%fused_computation.9 | convolution fusion | flops 2149842944 | bytes 8390656 | tf_op jit(solution)/shard_map/dot_general | solution.py:125
  381.2 7.4 %reshape.136 = bf16[16384,128]{1,0:T(8,128)(2,1)} reshape(bf16[512,4096]{1,0:T(8,128)(2,1)} %convolution_convert_fusion) | data formatting | bytes 8388608 | tf_op jit(solution)/shard_map/reshape | solution.py:129
  407.4 14.6 %psum.37 = f32[6,128]{1,0:T(8,128)S(1)} all-reduce(f32[6,128]{1,0:T(8,128)S(1)} %stack.126), channel_id=1, replica_groups=mesh['gx'=64,'gy'=8] {'gy'}, use_global_device_ids=true, to_apply=%region_18.19 | all-reduce | flops 768 | bytes 6144 | tf_op jit(solution)/shard_map/psum | solution.py:25
  434.6 4.1 collective-permute-start.54
  440.2 4.9 %collective-permute-start.55 = (f32[6,128]{1,0:T(8,128)S(1)}, f32[6,128]{1,0:T(8,128)S(1)}, u32[]{:S(2)}, u32[]{:S(2)}) collective-permute-start(f32[6,128]{1,0:T(8,128)S(1)} %add.249), channel_id=1, source_target_pairs={{0,64},{8,72},{16,80},{24,88},{32,96},{40,104},{48,112},{56,120},{... | collective-permute-start | bytes 9224 | tf_op jit(solution)/shard_map/ppermute | solution.py:33
  446.7 9.2 %collective-permute-start.56 = (f32[6,128]{1,0:T(8,128)S(1)}, f32[6,128]{1,0:T(8,128)S(1)}, u32[]{:S(2)}, u32[]{:S(2)}) collective-permute-start(f32[6,128]{1,0:T(8,128)S(1)} %add.250), channel_id=1, source_target_pairs={{0,128},{8,136},{16,144},{24,152},{32,160},{40,168},{48,176},{56,1... | collective-permute-start | bytes 9224 | tf_op jit(solution)/shard_map/ppermute | solution.py:33
  457.5 13.0 %collective-permute-start.57 = (f32[6,128]{1,0:T(8,128)S(1)}, f32[6,128]{1,0:T(8,128)S(1)}, u32[]{:S(2)}, u32[]{:S(2)}) collective-permute-start(f32[6,128]{1,0:T(8,128)S(1)} %add.251), channel_id=1, source_target_pairs={{0,256},{8,264},{16,272},{24,280},{32,288},{40,296},{48,304},{56,3... | collective-permute-start | bytes 9224 | tf_op jit(solution)/shard_map/ppermute | solution.py:33
  (173 shorter events, 170.4 us)
Async XLA Ops:
  7.2 160.9 %all-gather.3.cloned.1.call-start = ((), (), s32[]{:S(2)}) async-start(), calls=%async_computation | async-start | bytes 4718592 | tf_op jit(solution)/shard_map/all_gather | solution.py:55
  22.8 7.0 %collective-permute-start.12 = (f32[128]{0:T(128)S(1)}, f32[128]{0:T(128)S(1)}, u32[]{:S(2)}, u32[]{:S(2)}) collective-permute-start(f32[128]{0:T(128)S(1)} %psum.35), channel_id=1, source_target_pairs={{0,8},{8,0},{16,24},{24,16},{32,40},{40,32},{48,56},{56,48},{64,72... | collective-permute-start | bytes 1544 | tf_op jit(solution)/shard_map/ppermute | solution.py:33
  29.9 7.0 %collective-permute-start.13 = (f32[128]{0:T(128)S(1)}, f32[128]{0:T(128)S(1)}, u32[]{:S(2)}, u32[]{:S(2)}) collective-permute-start(f32[128]{0:T(128)S(1)} %add.219), channel_id=1, source_target_pairs={{0,16},{8,24},{16,0},{24,8},{32,48},{40,56},{48,32},{56,40},{64,80... | collective-permute-start | bytes 1544 | tf_op jit(solution)/shard_map/ppermute | solution.py:33
  42.3 6.3 %collective-permute-start.15 = (f32[128]{0:T(128)S(1)}, f32[128]{0:T(128)S(1)}, u32[]{:S(2)}, u32[]{:S(2)}) collective-permute-start(f32[128]{0:T(128)S(1)} %add.221), channel_id=1, source_target_pairs={{0,64},{8,72},{16,80},{24,88},{32,96},{40,104},{48,112},{56,120},{... | collective-permute-start | bytes 1544 | tf_op jit(solution)/shard_map/ppermute | solution.py:33
  48.6 9.4 %collective-permute-start.16 = (f32[128]{0:T(128)S(1)}, f32[128]{0:T(128)S(1)}, u32[]{:S(2)}, u32[]{:S(2)}) collective-permute-start(f32[128]{0:T(128)S(1)} %add.222), channel_id=1, source_target_pairs={{0,128},{8,136},{16,144},{24,152},{32,160},{40,168},{48,176},{56,1... | collective-permute-start | bytes 1544 | tf_op jit(solution)/shard_map/ppermute | solution.py:33
  58.0 15.6 %collective-permute-start.17 = (f32[128]{0:T(128)S(1)}, f32[128]{0:T(128)S(1)}, u32[]{:S(2)}, u32[]{:S(2)}) collective-permute-start(f32[128]{0:T(128)S(1)} %add.223), channel_id=1, source_target_pairs={{0,256},{8,264},{16,272},{24,280},{32,288},{40,296},{48,304},{56,3... | collective-permute-start | bytes 1544 | tf_op jit(solution)/shard_map/ppermute | solution.py:33
  74.6 14.3 %collective-permute-start.22 = (bf16[1,32,128]{2,1,0:T(8,128)(2,1)S(1)}, bf16[1,32,128]{2,1,0:T(8,128)(2,1)S(1)}, u32[]{:S(2)}, u32[]{:S(2)}) collective-permute-start(bf16[1,32,128]{2,1,0:T(8,128)(2,1)S(1)} %fusion.2), channel_id=1, source_target_pairs={{0,256},{8,264},{16,272},{24,280},{32,288},{40,296},{48,304},{56,3... | collective-permute-start | bytes 24584 | tf_op jit(solution)/shard_map/ppermute | solution.py:50
  88.9 9.5 %collective-permute-start.23 = (bf16[2,32,128]{2,1,0:T(8,128)(2,1)S(1)}, bf16[2,32,128]{2,1,0:T(8,128)(2,1)S(1)}, u32[]{:S(2)}, u32[]{:S(2)}) collective-permute-start(bf16[2,32,128]{2,1,0:T(8,128)(2,1)S(1)} %maximum_select_fusion.10), channel_id=1, source_target_pairs={{0,128},{8,136},{16,144},{24,152},{32,160},{40,168},{48,176},{56,1... | collective-permute-start | bytes 49160 | tf_op jit(solution)/shard_map/ppermute | solution.py:50
  98.5 6.7 %collective-permute-start.24 = (bf16[4,32,128]{2,1,0:T(8,128)(2,1)S(1)}, bf16[4,32,128]{2,1,0:T(8,128)(2,1)S(1)}, u32[]{:S(2)}, u32[]{:S(2)}) collective-permute-start(bf16[4,32,128]{2,1,0:T(8,128)(2,1)S(1)} %maximum_select_fusion.8), channel_id=1, source_target_pairs={{0,64},{8,72},{16,80},{24,88},{32,96},{40,104},{48,112},{56,120},{... | collective-permute-start | bytes 98312 | tf_op jit(solution)/shard_map/ppermute | solution.py:50
  111.4 8.5 %collective-permute-start.26 = (bf16[16,32,128]{2,1,0:T(8,128)(2,1)S(1)}, bf16[16,32,128]{2,1,0:T(8,128)(2,1)S(1)}, u32[]{:S(2)}, u32[]{:S(2)}) collective-permute-start(bf16[16,32,128]{2,1,0:T(8,128)(2,1)S(1)} %maximum_select_fusion.4), channel_id=1, source_target_pairs={{0,16},{8,24},{16,0},{24,8},{32,48},{40,56},{48,32},{56,40},{64,80... | collective-permute-start | bytes 393224 | tf_op jit(solution)/shard_map/ppermute | solution.py:50
  119.9 8.3 %collective-permute-start.27 = (bf16[32,32,128]{2,1,0:T(8,128)(2,1)S(1)}, bf16[32,32,128]{2,1,0:T(8,128)(2,1)S(1)}, u32[]{:S(2)}, u32[]{:S(2)}) collective-permute-start(bf16[32,32,128]{2,1,0:T(8,128)(2,1)S(1)} %maximum_select_fusion.2), channel_id=1, source_target_pairs={{0,8},{8,0},{16,24},{24,16},{32,40},{40,32},{48,56},{56,48},{64,72... | collective-permute-start | bytes 786440 | tf_op jit(solution)/shard_map/ppermute | solution.py:50
  129.1 238.1 %all-gather.5.cloned.1.call-start = ((), (), s32[]{:S(2)}) async-start(), calls=%async_computation.1 | async-start | bytes 4718592 | tf_op jit(solution)/shard_map/all_gather | solution.py:55
  130.9 12.0 %collective-permute-start.18 = (f32[128,128]{1,0:T(8,128)S(1)}, f32[128,128]{1,0:T(8,128)S(1)}, u32[]{:S(2)}, u32[]{:S(2)}) collective-permute-start(f32[128,128]{1,0:T(8,128)S(1)} %get-tuple-element.64), channel_id=1, source_target_pairs={{0,8},{8,16},{16,24},{24,32},{32,40},{40,48},{48,56},{56,64},{64,7... | collective-permute-start | bytes 196616 | tf_op jit(solution)/shard_map/ppermute | solution.py:15
  134.4 8.5 %collective-permute-start.20 = (f32[128,128]{1,0:T(8,128)S(1)}, f32[128,128]{1,0:T(8,128)S(1)}, u32[]{:S(2)}, u32[]{:S(2)}) collective-permute-start(f32[128,128]{1,0:T(8,128)S(1)} %get-tuple-element.65), channel_id=1, source_target_pairs={{0,1},{1,2},{2,3},{3,4},{4,5},{5,6},{6,7},{8,9},{9,10},{10,11},{11... | collective-permute-start | bytes 196616 | tf_op jit(solution)/shard_map/ppermute | solution.py:15
  135.7 7.2 %collective-permute-start.19 = (f32[128,128]{1,0:T(8,128)S(1)}, f32[128,128]{1,0:T(8,128)S(1)}, u32[]{:S(2)}, u32[]{:S(2)}) collective-permute-start(f32[128,128]{1,0:T(8,128)S(1)} %get-tuple-element.66), channel_id=1, source_target_pairs={{8,0},{16,8},{24,16},{32,24},{40,32},{48,40},{56,48},{64,56},{72,6... | collective-permute-start | bytes 196616 | tf_op jit(solution)/shard_map/ppermute | solution.py:15
  194.6 9.1 %collective-permute-start.28 = (bf16[128,128]{1,0:T(8,128)(2,1)S(1)}, bf16[128,128]{1,0:T(8,128)(2,1)S(1)}, u32[]{:S(2)}, u32[]{:S(2)}) collective-permute-start(bf16[128,128]{1,0:T(8,128)(2,1)S(1)} %get-tuple-element.72), channel_id=1, source_target_pairs={{0,8},{8,16},{16,24},{24,32},{32,40},{40,48},{48,56},{56,64},{64,7... | collective-permute-start | bytes 98312 | tf_op jit(solution)/shard_map/ppermute | solution.py:15
  228.5 7.0 %collective-permute-start.33 = (f32[3,128]{1,0:T(4,128)S(1)}, f32[3,128]{1,0:T(4,128)S(1)}, u32[]{:S(2)}, u32[]{:S(2)}) collective-permute-start(f32[3,128]{1,0:T(4,128)S(1)} %add.237), channel_id=1, source_target_pairs={{0,16},{8,24},{16,0},{24,8},{32,48},{40,56},{48,32},{56,40},{64,80... | collective-permute-start | bytes 4616 | tf_op jit(solution)/shard_map/ppermute | solution.py:33
  241.1 6.5 %collective-permute-start.35 = (f32[3,128]{1,0:T(4,128)S(1)}, f32[3,128]{1,0:T(4,128)S(1)}, u32[]{:S(2)}, u32[]{:S(2)}) collective-permute-start(f32[3,128]{1,0:T(4,128)S(1)} %add.239), channel_id=1, source_target_pairs={{0,64},{8,72},{16,80},{24,88},{32,96},{40,104},{48,112},{56,120},{... | collective-permute-start | bytes 4616 | tf_op jit(solution)/shard_map/ppermute | solution.py:33
  247.6 10.8 %collective-permute-start.36 = (f32[3,128]{1,0:T(4,128)S(1)}, f32[3,128]{1,0:T(4,128)S(1)}, u32[]{:S(2)}, u32[]{:S(2)}) collective-permute-start(f32[3,128]{1,0:T(4,128)S(1)} %add.240), channel_id=1, source_target_pairs={{0,128},{8,136},{16,144},{24,152},{32,160},{40,168},{48,176},{56,1... | collective-permute-start | bytes 4616 | tf_op jit(solution)/shard_map/ppermute | solution.py:33
  258.3 14.5 %collective-permute-start.37 = (f32[3,128]{1,0:T(4,128)S(1)}, f32[3,128]{1,0:T(4,128)S(1)}, u32[]{:S(2)}, u32[]{:S(2)}) collective-permute-start(f32[3,128]{1,0:T(4,128)S(1)} %add.241), channel_id=1, source_target_pairs={{0,256},{8,264},{16,272},{24,280},{32,288},{40,296},{48,304},{56,3... | collective-permute-start | bytes 4616 | tf_op jit(solution)/shard_map/ppermute | solution.py:33
  274.4 14.3 %collective-permute-start.42 = (bf16[1,32,128]{2,1,0:T(8,128)(2,1)S(1)}, bf16[1,32,128]{2,1,0:T(8,128)(2,1)S(1)}, u32[]{:S(2)}, u32[]{:S(2)}) collective-permute-start(bf16[1,32,128]{2,1,0:T(8,128)(2,1)S(1)} %fusion.3), channel_id=1, source_target_pairs={{0,256},{8,264},{16,272},{24,280},{32,288},{40,296},{48,304},{56,3... | collective-permute-start | bytes 24584 | tf_op jit(solution)/shard_map/ppermute | solution.py:50
  288.6 9.5 %collective-permute-start.43 = (bf16[2,32,128]{2,1,0:T(8,128)(2,1)S(1)}, bf16[2,32,128]{2,1,0:T(8,128)(2,1)S(1)}, u32[]{:S(2)}, u32[]{:S(2)}) collective-permute-start(bf16[2,32,128]{2,1,0:T(8,128)(2,1)S(1)} %maximum_select_fusion.11), channel_id=1, source_target_pairs={{0,128},{8,136},{16,144},{24,152},{32,160},{40,168},{48,176},{56,1... | collective-permute-start | bytes 49160 | tf_op jit(solution)/shard_map/ppermute | solution.py:50
  298.2 6.7 %collective-permute-start.44 = (bf16[4,32,128]{2,1,0:T(8,128)(2,1)S(1)}, bf16[4,32,128]{2,1,0:T(8,128)(2,1)S(1)}, u32[]{:S(2)}, u32[]{:S(2)}) collective-permute-start(bf16[4,32,128]{2,1,0:T(8,128)(2,1)S(1)} %maximum_select_fusion.9), channel_id=1, source_target_pairs={{0,64},{8,72},{16,80},{24,88},{32,96},{40,104},{48,112},{56,120},{... | collective-permute-start | bytes 98312 | tf_op jit(solution)/shard_map/ppermute | solution.py:50
  311.1 8.4 %collective-permute-start.46 = (bf16[16,32,128]{2,1,0:T(8,128)(2,1)S(1)}, bf16[16,32,128]{2,1,0:T(8,128)(2,1)S(1)}, u32[]{:S(2)}, u32[]{:S(2)}) collective-permute-start(bf16[16,32,128]{2,1,0:T(8,128)(2,1)S(1)} %maximum_select_fusion.5), channel_id=1, source_target_pairs={{0,16},{8,24},{16,0},{24,8},{32,48},{40,56},{48,32},{56,40},{64,80... | collective-permute-start | bytes 393224 | tf_op jit(solution)/shard_map/ppermute | solution.py:50
  319.5 8.3 %collective-permute-start.47 = (bf16[32,32,128]{2,1,0:T(8,128)(2,1)S(1)}, bf16[32,32,128]{2,1,0:T(8,128)(2,1)S(1)}, u32[]{:S(2)}, u32[]{:S(2)}) collective-permute-start(bf16[32,32,128]{2,1,0:T(8,128)(2,1)S(1)} %maximum_select_fusion.3), channel_id=1, source_target_pairs={{0,8},{8,0},{16,24},{24,16},{32,40},{40,32},{48,56},{56,48},{64,72... | collective-permute-start | bytes 786440 | tf_op jit(solution)/shard_map/ppermute | solution.py:50
  329.7 8.6 %collective-permute-start.38 = (f32[128,128]{1,0:T(8,128)S(1)}, f32[128,128]{1,0:T(8,128)S(1)}, u32[]{:S(2)}, u32[]{:S(2)}) collective-permute-start(f32[128,128]{1,0:T(8,128)S(1)} %get-tuple-element.60), channel_id=1, source_target_pairs={{0,8},{8,16},{16,24},{24,32},{32,40},{40,48},{48,56},{56,64},{64,7... | collective-permute-start | bytes 196616 | tf_op jit(solution)/shard_map/ppermute | solution.py:15
  331.9 6.5 %collective-permute-start.40 = (f32[128,128]{1,0:T(8,128)S(1)}, f32[128,128]{1,0:T(8,128)S(1)}, u32[]{:S(2)}, u32[]{:S(2)}) collective-permute-start(f32[128,128]{1,0:T(8,128)S(1)} %get-tuple-element.61), channel_id=1, source_target_pairs={{0,1},{1,2},{2,3},{3,4},{4,5},{5,6},{6,7},{8,9},{9,10},{10,11},{11... | collective-permute-start | bytes 196616 | tf_op jit(solution)/shard_map/ppermute | solution.py:15
  393.7 9.0 %collective-permute-start.48 = (bf16[128,128]{1,0:T(8,128)(2,1)S(1)}, bf16[128,128]{1,0:T(8,128)(2,1)S(1)}, u32[]{:S(2)}, u32[]{:S(2)}) collective-permute-start(bf16[128,128]{1,0:T(8,128)(2,1)S(1)} %get-tuple-element.68), channel_id=1, source_target_pairs={{0,8},{8,16},{16,24},{24,32},{32,40},{40,48},{48,56},{56,64},{64,7... | collective-permute-start | bytes 98312 | tf_op jit(solution)/shard_map/ppermute | solution.py:15
  427.6 7.0 %collective-permute-start.53 = (f32[6,128]{1,0:T(8,128)S(1)}, f32[6,128]{1,0:T(8,128)S(1)}, u32[]{:S(2)}, u32[]{:S(2)}) collective-permute-start(f32[6,128]{1,0:T(8,128)S(1)} %add.247), channel_id=1, source_target_pairs={{0,16},{8,24},{16,0},{24,8},{32,48},{40,56},{48,32},{56,40},{64,80... | collective-permute-start | bytes 9224 | tf_op jit(solution)/shard_map/ppermute | solution.py:33
  440.2 6.5 %collective-permute-start.55 = (f32[6,128]{1,0:T(8,128)S(1)}, f32[6,128]{1,0:T(8,128)S(1)}, u32[]{:S(2)}, u32[]{:S(2)}) collective-permute-start(f32[6,128]{1,0:T(8,128)S(1)} %add.249), channel_id=1, source_target_pairs={{0,64},{8,72},{16,80},{24,88},{32,96},{40,104},{48,112},{56,120},{... | collective-permute-start | bytes 9224 | tf_op jit(solution)/shard_map/ppermute | solution.py:33
  446.7 10.8 %collective-permute-start.56 = (f32[6,128]{1,0:T(8,128)S(1)}, f32[6,128]{1,0:T(8,128)S(1)}, u32[]{:S(2)}, u32[]{:S(2)}) collective-permute-start(f32[6,128]{1,0:T(8,128)S(1)} %add.250), channel_id=1, source_target_pairs={{0,128},{8,136},{16,144},{24,152},{32,160},{40,168},{48,176},{56,1... | collective-permute-start | bytes 9224 | tf_op jit(solution)/shard_map/ppermute | solution.py:33
  457.5 14.6 %collective-permute-start.57 = (f32[6,128]{1,0:T(8,128)S(1)}, f32[6,128]{1,0:T(8,128)S(1)}, u32[]{:S(2)}, u32[]{:S(2)}) collective-permute-start(f32[6,128]{1,0:T(8,128)S(1)} %add.251), channel_id=1, source_target_pairs={{0,256},{8,264},{16,272},{24,280},{32,288},{40,296},{48,304},{56,3... | collective-permute-start | bytes 9224 | tf_op jit(solution)/shard_map/ppermute | solution.py:33
  (25 other events, 741.4 us)
Sparse Core Ops, SparseCore 0:
  129.2 38.8 all-gather.2
  328.8 38.3 all-gather.4
where the time goes:
time: 484 us; the launch traced here: 482 us
  starting transfers between devices  210 us (43%)
  waiting for transfers between devices  139 us (29%)
  blocking collectives  43.9 us (9%)
  local copies, waits for them, and re-layouts  39 us (8%)
  matrix products  22.4 us (5%)
  between operations  16.4 us (3%)
  other arithmetic  10.6 us (2%)
    ppermute x18, starting transfers between devices, allsum(): lax.ppermute(value, axis, [(i, i ^ step) for i in range(count)])  110 us
    ppermute x12, starting transfers between devices, doubling_gather(): got = lax.ppermute(held, axis, [(i, i ^ step) for i in range(count)])  65.1 us
    all_gather x2, waiting for transfers between devices, doubling_gather(): lax.all_gather(held.reshape(-1, block.shape[-1]), 'gy', axis=0, tiled=True)  51.6 us
    psum x3, blocking collectives, allsum(): value = lax.psum(value, 'gy')  43.9 us
    ppermute x12, waiting for transfers between devices, doubling_gather(): got = lax.ppermute(held, axis, [(i, i ^ step) for i in range(count)])  41.3 us
    ppermute x18, waiting for transfers between devices, allsum(): lax.ppermute(value, axis, [(i, i ^ step) for i in range(count)])  40.5 us
    ppermute x16, starting transfers between devices, neighbours(): return (lax.ppermute(rows[1], axis, up), lax.ppermute(rows[0], axis, down))  35 us
    reshape x2, local copies, waits for them, and re-layouts, precondition(): placed.reshape(-1, system_count)  14.9 us
  transfers between devices with their start and end apart: 48, of which 36 were waited for; matrix products, arithmetic and copies ran while one was open for 1% of the time, Pallas kernels for 0%

commit v1 on v0

--- a/solution.py
+++ b/solution.py
@@ -6,6 +6,15 @@
 
 EPSILON = 1e-06
 KEPT_SHARE = 1.0 / 64
+_lift_rates = lambda mine: jnp.concatenate(
+    jax.lax.all_to_all(
+        jnp.stack([mine for _ in range(jax.lax.axis_size("gy"))]),
+        axis_name="gy",
+        split_axis=0,
+        concat_axis=0,
+    ),
+    axis=0,
+)
 
 
 def neighbours(rows, axis):
@@ -52,7 +61,7 @@
         held = jnp.where(
             upper, jnp.concatenate([got, held], axis=0), jnp.concatenate([held, got], axis=0)
         )
-    return lax.all_gather(held.reshape(-1, block.shape[-1]), "gy", axis=0, tiled=True)
+    return _lift_rates(held.reshape(-1, block.shape[-1]))
 
 
 def gathered_order(rounds, count_y):

time: 484 us -> 508 us (1.050)
  the two profiles are of different devices: /device:TPU:8 before, /device:TPU:384 now
where the time goes in v1:
time: 508 us; the launch traced here: 506 us
  waiting for transfers between devices  243 us (48%)
  starting transfers between devices  145 us (29%)
  local copies, waits for them, and re-layouts  44 us (9%)
  blocking collectives  39.4 us (8%)
  matrix products  22.3 us (4%)
  other arithmetic  8.34 us (2%)
    ppermute x18, waiting for transfers between devices, allsum(): lax.ppermute(value, axis, [(i, i ^ step) for i in range(count)])  91.6 us
    ppermute x12, waiting for transfers between devices, doubling_gather(): got = lax.ppermute(held, axis, [(i, i ^ step) for i in range(count)])  68.5 us
    all_to_all x2, waiting for transfers between devices, jax.lax.all_to_all(jnp.stack([mine for _ in range(jax.lax.axis_size('gy')...  61 us
    ppermute x18, starting transfers between devices, allsum(): lax.ppermute(value, axis, [(i, i ^ step) for i in range(count)])  51.8 us
    ppermute x16, starting transfers between devices, neighbours(): return (lax.ppermute(rows[1], axis, up), lax.ppermute(rows[0], axis, down))  46 us
    psum x3, blocking collectives, allsum(): value = lax.psum(value, 'gy')  39.4 us
    ppermute x12, starting transfers between devices, doubling_gather(): got = lax.ppermute(held, axis, [(i, i ^ step) for i in range(count)])  38.3 us
    ppermute x16, waiting for transfers between devices, neighbours(): return (lax.ppermute(rows[1], axis, up), lax.ppermute(rows[0], axis, down))  22.3 us
  transfers between devices with their start and end apart: 48, of which 37 were waited for; matrix products, arithmetic and copies ran while one was open for 1% of the time, Pallas kernels for 0%

profile of v1, /device:TPU:384, one launch (start us, length us, event | category | flops | bytes accessed | tf_op | source)
XLA Modules:
  0.0 505.8 jit_solution(14532662825605448992)
XLA Ops:
  1.6 14.6 %psum.35 = f32[128]{0:T(128)S(1)} all-reduce(f32[128]{0:T(128)S(1)} %multiply_reduce_fusion.10), channel_id=1, replica_groups=mesh['gx'=64,'gy'=8] {'gy'}, use_global_device_ids=true, to_apply=%region_1.0 | all-reduce | flops 128 | bytes 1024 | tf_op jit(solution)/shard_map/psum | solution.py:34
  21.7 5.1 %collective-permute-start.13 = (f32[128]{0:T(128)S(1)}, f32[128]{0:T(128)S(1)}, u32[]{:S(2)}, u32[]{:S(2)}) collective-permute-start(f32[128]{0:T(128)S(1)} %add.219), channel_id=1, source_target_pairs={{0,16},{8,24},{16,0},{24,8},{32,48},{40,56},{48,32},{56,40},{64,80... | collective-permute-start | bytes 1544 | tf_op jit(solution)/shard_map/ppermute | solution.py:42
  40.4 5.4 %collective-permute-start.16 = (f32[128]{0:T(128)S(1)}, f32[128]{0:T(128)S(1)}, u32[]{:S(2)}, u32[]{:S(2)}) collective-permute-start(f32[128]{0:T(128)S(1)} %add.222), channel_id=1, source_target_pairs={{0,128},{8,136},{16,144},{24,152},{32,160},{40,168},{48,176},{56,1... | collective-permute-start | bytes 1544 | tf_op jit(solution)/shard_map/ppermute | solution.py:42
  53.8 10.2 %collective-permute-done.17 = f32[128]{0:T(128)S(1)} collective-permute-done((f32[128]{0:T(128)S(1)}, f32[128]{0:T(128)S(1)}, u32[]{:S(2)}, u32[]{:S(2)}) %collective-permute-start.17) | collective-permute-done | bytes 544 | tf_op jit(solution)/shard_map/ppermute | solution.py:42
  69.0 10.2 %collective-permute-done.22 = bf16[1,32,128]{2,1,0:T(8,128)(2,1)S(1)} collective-permute-done((bf16[1,32,128]{2,1,0:T(8,128)(2,1)S(1)}, bf16[1,32,128]{2,1,0:T(8,128)(2,1)S(1)}, u32[]{:S(2)}, u32[]{:S(2)}) %collective-permute-start.22) | collective-permute-done | bytes 8224 | tf_op jit(solution)/shard_map/ppermute | solution.py:59
  79.2 5.4 %collective-permute-start.23 = (bf16[2,32,128]{2,1,0:T(8,128)(2,1)S(1)}, bf16[2,32,128]{2,1,0:T(8,128)(2,1)S(1)}, u32[]{:S(2)}, u32[]{:S(2)}) collective-permute-start(bf16[2,32,128]{2,1,0:T(8,128)(2,1)S(1)} %maximum_select_fusion.10), channel_id=1, source_target_pairs={{0,128},{8,136},{16,144},{24,152},{32,160},{40,168},{48,176},{56,1... | collective-permute-start | bytes 49160 | tf_op jit(solution)/shard_map/ppermute | solution.py:59
  101.7 5.1 %collective-permute-start.26 = (bf16[16,32,128]{2,1,0:T(8,128)(2,1)S(1)}, bf16[16,32,128]{2,1,0:T(8,128)(2,1)S(1)}, u32[]{:S(2)}, u32[]{:S(2)}) collective-permute-start(bf16[16,32,128]{2,1,0:T(8,128)(2,1)S(1)} %maximum_select_fusion.4), channel_id=1, source_target_pairs={{0,16},{8,24},{16,0},{24,8},{32,48},{40,56},{48,32},{56,40},{64,80... | collective-permute-start | bytes 393224 | tf_op jit(solution)/shard_map/ppermute | solution.py:59
  131.2 6.6 %collective-permute-start.19 = (f32[128,128]{1,0:T(8,128)S(1)}, f32[128,128]{1,0:T(8,128)S(1)}, u32[]{:S(2)}, u32[]{:S(2)}) collective-permute-start(f32[128,128]{1,0:T(8,128)S(1)} %get-tuple-element.66), channel_id=1, source_target_pairs={{8,0},{16,8},{24,16},{32,24},{40,32},{48,40},{56,48},{64,56},{72,6... | collective-permute-start | bytes 196616 | tf_op jit(solution)/shard_map/ppermute | solution.py:24
  147.9 28.0 %all-to-all-done = bf16[8,2048,128]{2,1,0:T(8,128)(2,1)} async-done(((bf16[8,2048,128]{2,1,0:T(8,128)(2,1)}), bf16[8,2048,128]{2,1,0:T(8,128)(2,1)}, u32[]{:S(2)}, u32[]{:S(2)}) %all-to-all-start) | async-done | bytes 4194336 | tf_op jit(solution)/shard_map/all_to_all | solution.py:10
  175.9 7.3 %reshape_reshape.6 = bf16[512,4096]{1,0:T(8,128)(2,1)} reshape(bf16[8,2048,128]{2,1,0:T(8,128)(2,1)} %all-to-all-done) | data formatting | bytes 8388608 | tf_op jit(solution)/shard_map/reshape;reshape | solution.py:133
  183.2 6.6 %convolution_convert_fusion.1 = bf16[512,4096]{1,0:T(8,128)(2,1)} fusion(bf16[512,4096]{1,0:T(8,128)(2,1)} %reshape_reshape.6, s32[512]{0:T(512)S(1)} %gather_fusion.1), kind=kOutput, calls=%fused_computation.10 | convolution fusion | flops 2149842944 | bytes 8390656 | tf_op jit(solution)/shard_map/dot_general | solution.py:134
  189.8 7.5 %reshape.130 = bf16[16384,128]{1,0:T(8,128)(2,1)} reshape(bf16[512,4096]{1,0:T(8,128)(2,1)} %convolution_convert_fusion.1) | data formatting | bytes 8388608 | tf_op jit(solution)/shard_map/reshape | solution.py:138
  206.8 6.6 %collective-permute-start.29 = (bf16[128,128]{1,0:T(8,128)(2,1)S(1)}, bf16[128,128]{1,0:T(8,128)(2,1)S(1)}, u32[]{:S(2)}, u32[]{:S(2)}) collective-permute-start(bf16[128,128]{1,0:T(8,128)(2,1)S(1)} %get-tuple-element.74), channel_id=1, source_target_pairs={{8,0},{16,8},{24,16},{32,24},{40,32},{48,40},{56,48},{64,56},{72,6... | collective-permute-start | bytes 98312 | tf_op jit(solution)/shard_map/ppermute | solution.py:24
  215.3 7.2 %collective-permute-done.28 = bf16[128,128]{1,0:T(8,128)(2,1)S(1)} collective-permute-done((bf16[128,128]{1,0:T(8,128)(2,1)S(1)}, bf16[128,128]{1,0:T(8,128)(2,1)S(1)}, u32[]{:S(2)}, u32[]{:S(2)}) %collective-permute-start.28) | collective-permute-done | bytes 32800 | tf_op jit(solution)/shard_map/ppermute | solution.py:24
  225.1 12.4 %psum.36 = f32[3,128]{1,0:T(4,128)S(1)} all-reduce(f32[3,128]{1,0:T(4,128)S(1)} %pad_maximum_fusion.4), channel_id=1, replica_groups=mesh['gx'=64,'gy'=8] {'gy'}, use_global_device_ids=true, to_apply=%region_6.7 | all-reduce | flops 384 | bytes 3072 | tf_op jit(solution)/shard_map/psum | solution.py:34
  244.9 5.1 collective-permute-done.33
  265.5 5.7 %collective-permute-done.36 = f32[3,128]{1,0:T(4,128)S(1)} collective-permute-done((f32[3,128]{1,0:T(4,128)S(1)}, f32[3,128]{1,0:T(4,128)S(1)}, u32[]{:S(2)}, u32[]{:S(2)}) %collective-permute-start.36) | collective-permute-done | bytes 1568 | tf_op jit(solution)/shard_map/ppermute | solution.py:42
  274.0 11.4 %collective-permute-done.37 = f32[3,128]{1,0:T(4,128)S(1)} collective-permute-done((f32[3,128]{1,0:T(4,128)S(1)}, f32[3,128]{1,0:T(4,128)S(1)}, u32[]{:S(2)}, u32[]{:S(2)}) %collective-permute-start.37) | collective-permute-done | bytes 1568 | tf_op jit(solution)/shard_map/ppermute | solution.py:42
  289.7 11.9 %collective-permute-done.42 = bf16[1,32,128]{2,1,0:T(8,128)(2,1)S(1)} collective-permute-done((bf16[1,32,128]{2,1,0:T(8,128)(2,1)S(1)}, bf16[1,32,128]{2,1,0:T(8,128)(2,1)S(1)}, u32[]{:S(2)}, u32[]{:S(2)}) %collective-permute-start.42) | collective-permute-done | bytes 8224 | tf_op jit(solution)/shard_map/ppermute | solution.py:59
  304.8 6.4 %collective-permute-done.43 = bf16[2,32,128]{2,1,0:T(8,128)(2,1)S(1)} collective-permute-done((bf16[2,32,128]{2,1,0:T(8,128)(2,1)S(1)}, bf16[2,32,128]{2,1,0:T(8,128)(2,1)S(1)}, u32[]{:S(2)}, u32[]{:S(2)}) %collective-permute-start.43) | collective-permute-done | bytes 16416 | tf_op jit(solution)/shard_map/ppermute | solution.py:59
  326.0 6.4 %collective-permute-done.46 = bf16[16,32,128]{2,1,0:T(8,128)(2,1)S(1)} collective-permute-done((bf16[16,32,128]{2,1,0:T(8,128)(2,1)S(1)}, bf16[16,32,128]{2,1,0:T(8,128)(2,1)S(1)}, u32[]{:S(2)}, u32[]{:S(2)}) %collective-permute-start.46) | collective-permute-done | bytes 131104 | tf_op jit(solution)/shard_map/ppermute | solution.py:59
  334.6 6.2 %collective-permute-done.47 = bf16[32,32,128]{2,1,0:T(8,128)(2,1)S(1)} collective-permute-done((bf16[32,32,128]{2,1,0:T(8,128)(2,1)S(1)}, bf16[32,32,128]{2,1,0:T(8,128)(2,1)S(1)}, u32[]{:S(2)}, u32[]{:S(2)}) %collective-permute-start.47) | collective-permute-done | bytes 262176 | tf_op jit(solution)/shard_map/ppermute | solution.py:59
  359.6 5.2 %collective-permute-done.38 = f32[128,128]{1,0:T(8,128)S(1)} collective-permute-done((f32[128,128]{1,0:T(8,128)S(1)}, f32[128,128]{1,0:T(8,128)S(1)}, u32[]{:S(2)}, u32[]{:S(2)}) %collective-permute-start.38) | collective-permute-done | bytes 65568 | tf_op jit(solution)/shard_map/ppermute | solution.py:24
  365.2 33.0 %all-to-all-done.1 = bf16[8,2048,128]{2,1,0:T(8,128)(2,1)} async-done(((bf16[8,2048,128]{2,1,0:T(8,128)(2,1)}), bf16[8,2048,128]{2,1,0:T(8,128)(2,1)}, u32[]{:S(2)}, u32[]{:S(2)}) %all-to-all-start.1) | async-done | bytes 4194336 | tf_op jit(solution)/shard_map/all_to_all | solution.py:10
  398.2 7.3 %reshape_reshape.7 = bf16[512,4096]{1,0:T(8,128)(2,1)} reshape(bf16[8,2048,128]{2,1,0:T(8,128)(2,1)} %all-to-all-done.1) | data formatting | bytes 8388608 | tf_op jit(solution)/shard_map/reshape;reshape | solution.py:133
  405.5 6.6 %convolution_convert_fusion = bf16[512,4096]{1,0:T(8,128)(2,1)} fusion(bf16[512,4096]{1,0:T(8,128)(2,1)} %reshape_reshape.7, s32[512]{0:T(512)S(1)} %gather_fusion.1), kind=kOutput, calls=%fused_computation.9 | convolution fusion | flops 2149842944 | bytes 8390656 | tf_op jit(solution)/shard_map/dot_general | solution.py:134
  412.1 7.4 %reshape.132 = bf16[16384,128]{1,0:T(8,128)(2,1)} reshape(bf16[512,4096]{1,0:T(8,128)(2,1)} %convolution_convert_fusion) | data formatting | bytes 8388608 | tf_op jit(solution)/shard_map/reshape | solution.py:138
  434.9 5.2 %collective-permute-done.48 = bf16[128,128]{1,0:T(8,128)(2,1)S(1)} collective-permute-done((bf16[128,128]{1,0:T(8,128)(2,1)S(1)}, bf16[128,128]{1,0:T(8,128)(2,1)S(1)}, u32[]{:S(2)}, u32[]{:S(2)}) %collective-permute-start.48) | collective-permute-done | bytes 32800 | tf_op jit(solution)/shard_map/ppermute | solution.py:24
  442.7 12.4 %psum.37 = f32[6,128]{1,0:T(8,128)S(1)} all-reduce(f32[6,128]{1,0:T(8,128)S(1)} %stack.134), channel_id=1, replica_groups=mesh['gx'=64,'gy'=8] {'gy'}, use_global_device_ids=true, to_apply=%region_18.19 | all-reduce | flops 768 | bytes 6144 | tf_op jit(solution)/shard_map/psum | solution.py:34
  462.5 5.1 %collective-permute-done.53 = f32[6,128]{1,0:T(8,128)S(1)} collective-permute-done((f32[6,128]{1,0:T(8,128)S(1)}, f32[6,128]{1,0:T(8,128)S(1)}, u32[]{:S(2)}, u32[]{:S(2)}) %collective-permute-start.53) | collective-permute-done | bytes 3104 | tf_op jit(solution)/shard_map/ppermute | solution.py:42
  482.9 5.9 %collective-permute-done.56 = f32[6,128]{1,0:T(8,128)S(1)} collective-permute-done((f32[6,128]{1,0:T(8,128)S(1)}, f32[6,128]{1,0:T(8,128)S(1)}, u32[]{:S(2)}, u32[]{:S(2)}) %collective-permute-start.56) | collective-permute-done | bytes 3104 | tf_op jit(solution)/shard_map/ppermute | solution.py:42
  491.3 11.8 %collective-permute-done.57 = f32[6,128]{1,0:T(8,128)S(1)} collective-permute-done((f32[6,128]{1,0:T(8,128)S(1)}, f32[6,128]{1,0:T(8,128)S(1)}, u32[]{:S(2)}, u32[]{:S(2)}) %collective-permute-start.57) | collective-permute-done | bytes 3104 | tf_op jit(solution)/shard_map/ppermute | solution.py:42
  (173 shorter events, 211.7 us)
Async XLA Ops:
  40.4 9.4 %collective-permute-start.16 = (f32[128]{0:T(128)S(1)}, f32[128]{0:T(128)S(1)}, u32[]{:S(2)}, u32[]{:S(2)}) collective-permute-start(f32[128]{0:T(128)S(1)} %add.222), channel_id=1, source_target_pairs={{0,128},{8,136},{16,144},{24,152},{32,160},{40,168},{48,176},{56,1... | collective-permute-start | bytes 1544 | tf_op jit(solution)/shard_map/ppermute | solution.py:42
  49.8 14.2 %collective-permute-start.17 = (f32[128]{0:T(128)S(1)}, f32[128]{0:T(128)S(1)}, u32[]{:S(2)}, u32[]{:S(2)}) collective-permute-start(f32[128]{0:T(128)S(1)} %add.223), channel_id=1, source_target_pairs={{0,256},{8,264},{16,272},{24,280},{32,288},{40,296},{48,304},{56,3... | collective-permute-start | bytes 1544 | tf_op jit(solution)/shard_map/ppermute | solution.py:42
  65.0 14.3 %collective-permute-start.22 = (bf16[1,32,128]{2,1,0:T(8,128)(2,1)S(1)}, bf16[1,32,128]{2,1,0:T(8,128)(2,1)S(1)}, u32[]{:S(2)}, u32[]{:S(2)}) collective-permute-start(bf16[1,32,128]{2,1,0:T(8,128)(2,1)S(1)} %fusion.2), channel_id=1, source_target_pairs={{0,256},{8,264},{16,272},{24,280},{32,288},{40,296},{48,304},{56,3... | collective-permute-start | bytes 24584 | tf_op jit(solution)/shard_map/ppermute | solution.py:59
  79.2 9.5 %collective-permute-start.23 = (bf16[2,32,128]{2,1,0:T(8,128)(2,1)S(1)}, bf16[2,32,128]{2,1,0:T(8,128)(2,1)S(1)}, u32[]{:S(2)}, u32[]{:S(2)}) collective-permute-start(bf16[2,32,128]{2,1,0:T(8,128)(2,1)S(1)} %maximum_select_fusion.10), channel_id=1, source_target_pairs={{0,128},{8,136},{16,144},{24,152},{32,160},{40,168},{48,176},{56,1... | collective-permute-start | bytes 49160 | tf_op jit(solution)/shard_map/ppermute | solution.py:59
  101.7 8.4 %collective-permute-start.26 = (bf16[16,32,128]{2,1,0:T(8,128)(2,1)S(1)}, bf16[16,32,128]{2,1,0:T(8,128)(2,1)S(1)}, u32[]{:S(2)}, u32[]{:S(2)}) collective-permute-start(bf16[16,32,128]{2,1,0:T(8,128)(2,1)S(1)} %maximum_select_fusion.4), channel_id=1, source_target_pairs={{0,16},{8,24},{16,0},{24,8},{32,48},{40,56},{48,32},{56,40},{64,80... | collective-permute-start | bytes 393224 | tf_op jit(solution)/shard_map/ppermute | solution.py:59
  110.0 8.3 %collective-permute-start.27 = (bf16[32,32,128]{2,1,0:T(8,128)(2,1)S(1)}, bf16[32,32,128]{2,1,0:T(8,128)(2,1)S(1)}, u32[]{:S(2)}, u32[]{:S(2)}) collective-permute-start(bf16[32,32,128]{2,1,0:T(8,128)(2,1)S(1)} %maximum_select_fusion.2), channel_id=1, source_target_pairs={{0,8},{8,0},{16,24},{24,16},{32,40},{40,32},{48,56},{56,48},{64,72... | collective-permute-start | bytes 786440 | tf_op jit(solution)/shard_map/ppermute | solution.py:59
  121.0 54.9 %all-to-all-start = ((bf16[8,2048,128]{2,1,0:T(8,128)(2,1)}), bf16[8,2048,128]{2,1,0:T(8,128)(2,1)}, u32[]{:S(2)}, u32[]{:S(2)}) async-start(bf16[8,2048,128]{2,1,0:T(8,128)(2,1)} %stack.107), calls=%async_computation | async-start | bytes 8388608 | tf_op jit(solution)/shard_map/all_to_all | solution.py:10
  126.8 16.4 %collective-permute-start.21 = (f32[128,128]{1,0:T(8,128)S(1)}, f32[128,128]{1,0:T(8,128)S(1)}, u32[]{:S(2)}, u32[]{:S(2)}) collective-permute-start(f32[128,128]{1,0:T(8,128)S(1)} %get-tuple-element.67), channel_id=1, source_target_pairs={{1,0},{2,1},{3,2},{4,3},{5,4},{6,5},{7,6},{9,8},{10,9},{11,10},{12... | collective-permute-start | bytes 196616 | tf_op jit(solution)/shard_map/ppermute | solution.py:24
  128.1 15.1 %collective-permute-start.20 = (f32[128,128]{1,0:T(8,128)S(1)}, f32[128,128]{1,0:T(8,128)S(1)}, u32[]{:S(2)}, u32[]{:S(2)}) collective-permute-start(f32[128,128]{1,0:T(8,128)S(1)} %get-tuple-element.65), channel_id=1, source_target_pairs={{0,1},{1,2},{2,3},{3,4},{4,5},{5,6},{6,7},{8,9},{9,10},{10,11},{11... | collective-permute-start | bytes 196616 | tf_op jit(solution)/shard_map/ppermute | solution.py:24
  131.2 12.1 %collective-permute-start.19 = (f32[128,128]{1,0:T(8,128)S(1)}, f32[128,128]{1,0:T(8,128)S(1)}, u32[]{:S(2)}, u32[]{:S(2)}) collective-permute-start(f32[128,128]{1,0:T(8,128)S(1)} %get-tuple-element.66), channel_id=1, source_target_pairs={{8,0},{16,8},{24,16},{32,24},{40,32},{48,40},{56,48},{64,56},{72,6... | collective-permute-start | bytes 196616 | tf_op jit(solution)/shard_map/ppermute | solution.py:24
  137.7 9.8 %collective-permute-start.18 = (f32[128,128]{1,0:T(8,128)S(1)}, f32[128,128]{1,0:T(8,128)S(1)}, u32[]{:S(2)}, u32[]{:S(2)}) collective-permute-start(f32[128,128]{1,0:T(8,128)S(1)} %get-tuple-element.64), channel_id=1, source_target_pairs={{0,8},{8,16},{16,24},{24,32},{32,40},{40,48},{48,56},{56,64},{64,7... | collective-permute-start | bytes 196616 | tf_op jit(solution)/shard_map/ppermute | solution.py:24
  202.4 12.9 %collective-permute-start.31 = (bf16[128,128]{1,0:T(8,128)(2,1)S(1)}, bf16[128,128]{1,0:T(8,128)(2,1)S(1)}, u32[]{:S(2)}, u32[]{:S(2)}) collective-permute-start(bf16[128,128]{1,0:T(8,128)(2,1)S(1)} %get-tuple-element.75), channel_id=1, source_target_pairs={{1,0},{2,1},{3,2},{4,3},{5,4},{6,5},{7,6},{9,8},{10,9},{11,10},{12... | collective-permute-start | bytes 98312 | tf_op jit(solution)/shard_map/ppermute | solution.py:24
  203.7 11.6 %collective-permute-start.30 = (bf16[128,128]{1,0:T(8,128)(2,1)S(1)}, bf16[128,128]{1,0:T(8,128)(2,1)S(1)}, u32[]{:S(2)}, u32[]{:S(2)}) collective-permute-start(bf16[128,128]{1,0:T(8,128)(2,1)S(1)} %get-tuple-element.73), channel_id=1, source_target_pairs={{0,1},{1,2},{2,3},{3,4},{4,5},{5,6},{6,7},{8,9},{9,10},{10,11},{11... | collective-permute-start | bytes 98312 | tf_op jit(solution)/shard_map/ppermute | solution.py:24
  206.8 8.6 %collective-permute-start.29 = (bf16[128,128]{1,0:T(8,128)(2,1)S(1)}, bf16[128,128]{1,0:T(8,128)(2,1)S(1)}, u32[]{:S(2)}, u32[]{:S(2)}) collective-permute-start(bf16[128,128]{1,0:T(8,128)(2,1)S(1)} %get-tuple-element.74), channel_id=1, source_target_pairs={{8,0},{16,8},{24,16},{32,24},{40,32},{48,40},{56,48},{64,56},{72,6... | collective-permute-start | bytes 98312 | tf_op jit(solution)/shard_map/ppermute | solution.py:24
  213.3 9.1 %collective-permute-start.28 = (bf16[128,128]{1,0:T(8,128)(2,1)S(1)}, bf16[128,128]{1,0:T(8,128)(2,1)S(1)}, u32[]{:S(2)}, u32[]{:S(2)}) collective-permute-start(bf16[128,128]{1,0:T(8,128)(2,1)S(1)} %get-tuple-element.72), channel_id=1, source_target_pairs={{0,8},{8,16},{16,24},{24,32},{32,40},{40,48},{48,56},{56,64},{64,7... | collective-permute-start | bytes 98312 | tf_op jit(solution)/shard_map/ppermute | solution.py:24
  243.0 7.0 %collective-permute-start.33 = (f32[3,128]{1,0:T(4,128)S(1)}, f32[3,128]{1,0:T(4,128)S(1)}, u32[]{:S(2)}, u32[]{:S(2)}) collective-permute-start(f32[3,128]{1,0:T(4,128)S(1)} %add.237), channel_id=1, source_target_pairs={{0,16},{8,24},{16,0},{24,8},{32,48},{40,56},{48,32},{56,40},{64,80... | collective-permute-start | bytes 4616 | tf_op jit(solution)/shard_map/ppermute | solution.py:42
  261.8 9.4 %collective-permute-start.36 = (f32[3,128]{1,0:T(4,128)S(1)}, f32[3,128]{1,0:T(4,128)S(1)}, u32[]{:S(2)}, u32[]{:S(2)}) collective-permute-start(f32[3,128]{1,0:T(4,128)S(1)} %add.240), channel_id=1, source_target_pairs={{0,128},{8,136},{16,144},{24,152},{32,160},{40,168},{48,176},{56,1... | collective-permute-start | bytes 4616 | tf_op jit(solution)/shard_map/ppermute | solution.py:42
  271.2 14.2 %collective-permute-start.37 = (f32[3,128]{1,0:T(4,128)S(1)}, f32[3,128]{1,0:T(4,128)S(1)}, u32[]{:S(2)}, u32[]{:S(2)}) collective-permute-start(f32[3,128]{1,0:T(4,128)S(1)} %add.241), channel_id=1, source_target_pairs={{0,256},{8,264},{16,272},{24,280},{32,288},{40,296},{48,304},{56,3... | collective-permute-start | bytes 4616 | tf_op jit(solution)/shard_map/ppermute | solution.py:42
  286.9 14.6 %collective-permute-start.42 = (bf16[1,32,128]{2,1,0:T(8,128)(2,1)S(1)}, bf16[1,32,128]{2,1,0:T(8,128)(2,1)S(1)}, u32[]{:S(2)}, u32[]{:S(2)}) collective-permute-start(bf16[1,32,128]{2,1,0:T(8,128)(2,1)S(1)} %fusion.3), channel_id=1, source_target_pairs={{0,256},{8,264},{16,272},{24,280},{32,288},{40,296},{48,304},{56,3... | collective-permute-start | bytes 24584 | tf_op jit(solution)/shard_map/ppermute | solution.py:59
  301.5 9.6 %collective-permute-start.43 = (bf16[2,32,128]{2,1,0:T(8,128)(2,1)S(1)}, bf16[2,32,128]{2,1,0:T(8,128)(2,1)S(1)}, u32[]{:S(2)}, u32[]{:S(2)}) collective-permute-start(bf16[2,32,128]{2,1,0:T(8,128)(2,1)S(1)} %maximum_select_fusion.11), channel_id=1, source_target_pairs={{0,128},{8,136},{16,144},{24,152},{32,160},{40,168},{48,176},{56,1... | collective-permute-start | bytes 49160 | tf_op jit(solution)/shard_map/ppermute | solution.py:59
  324.1 8.4 %collective-permute-start.46 = (bf16[16,32,128]{2,1,0:T(8,128)(2,1)S(1)}, bf16[16,32,128]{2,1,0:T(8,128)(2,1)S(1)}, u32[]{:S(2)}, u32[]{:S(2)}) collective-permute-start(bf16[16,32,128]{2,1,0:T(8,128)(2,1)S(1)} %maximum_select_fusion.5), channel_id=1, source_target_pairs={{0,16},{8,24},{16,0},{24,8},{32,48},{40,56},{48,32},{56,40},{64,80... | collective-permute-start | bytes 393224 | tf_op jit(solution)/shard_map/ppermute | solution.py:59
  332.5 8.3 %collective-permute-start.47 = (bf16[32,32,128]{2,1,0:T(8,128)(2,1)S(1)}, bf16[32,32,128]{2,1,0:T(8,128)(2,1)S(1)}, u32[]{:S(2)}, u32[]{:S(2)}) collective-permute-start(bf16[32,32,128]{2,1,0:T(8,128)(2,1)S(1)} %maximum_select_fusion.3), channel_id=1, source_target_pairs={{0,8},{8,0},{16,24},{24,16},{32,40},{40,32},{48,56},{56,48},{64,72... | collective-permute-start | bytes 786440 | tf_op jit(solution)/shard_map/ppermute | solution.py:59
  343.4 54.8 %all-to-all-start.1 = ((bf16[8,2048,128]{2,1,0:T(8,128)(2,1)}), bf16[8,2048,128]{2,1,0:T(8,128)(2,1)}, u32[]{:S(2)}, u32[]{:S(2)}) async-start(bf16[8,2048,128]{2,1,0:T(8,128)(2,1)} %stack.123), calls=%async_computation.1 | async-start | bytes 8388608 | tf_op jit(solution)/shard_map/all_to_all | solution.py:10
  349.0 10.2 %collective-permute-start.41 = (f32[128,128]{1,0:T(8,128)S(1)}, f32[128,128]{1,0:T(8,128)S(1)}, u32[]{:S(2)}, u32[]{:S(2)}) collective-permute-start(f32[128,128]{1,0:T(8,128)S(1)} %get-tuple-element.63), channel_id=1, source_target_pairs={{1,0},{2,1},{3,2},{4,3},{5,4},{6,5},{7,6},{9,8},{10,9},{11,10},{12... | collective-permute-start | bytes 196616 | tf_op jit(solution)/shard_map/ppermute | solution.py:24
  350.3 8.9 %collective-permute-start.40 = (f32[128,128]{1,0:T(8,128)S(1)}, f32[128,128]{1,0:T(8,128)S(1)}, u32[]{:S(2)}, u32[]{:S(2)}) collective-permute-start(f32[128,128]{1,0:T(8,128)S(1)} %get-tuple-element.61), channel_id=1, source_target_pairs={{0,1},{1,2},{2,3},{3,4},{4,5},{5,6},{6,7},{8,9},{9,10},{10,11},{11... | collective-permute-start | bytes 196616 | tf_op jit(solution)/shard_map/ppermute | solution.py:24
  355.3 9.5 %collective-permute-start.38 = (f32[128,128]{1,0:T(8,128)S(1)}, f32[128,128]{1,0:T(8,128)S(1)}, u32[]{:S(2)}, u32[]{:S(2)}) collective-permute-start(f32[128,128]{1,0:T(8,128)S(1)} %get-tuple-element.60), channel_id=1, source_target_pairs={{0,8},{8,16},{16,24},{24,32},{32,40},{40,48},{48,56},{56,64},{64,7... | collective-permute-start | bytes 196616 | tf_op jit(solution)/shard_map/ppermute | solution.py:24
  424.6 10.2 %collective-permute-start.51 = (bf16[128,128]{1,0:T(8,128)(2,1)S(1)}, bf16[128,128]{1,0:T(8,128)(2,1)S(1)}, u32[]{:S(2)}, u32[]{:S(2)}) collective-permute-start(bf16[128,128]{1,0:T(8,128)(2,1)S(1)} %get-tuple-element.71), channel_id=1, source_target_pairs={{1,0},{2,1},{3,2},{4,3},{5,4},{6,5},{7,6},{9,8},{10,9},{11,10},{12... | collective-permute-start | bytes 98312 | tf_op jit(solution)/shard_map/ppermute | solution.py:24
  425.9 8.9 %collective-permute-start.50 = (bf16[128,128]{1,0:T(8,128)(2,1)S(1)}, bf16[128,128]{1,0:T(8,128)(2,1)S(1)}, u32[]{:S(2)}, u32[]{:S(2)}) collective-permute-start(bf16[128,128]{1,0:T(8,128)(2,1)S(1)} %get-tuple-element.69), channel_id=1, source_target_pairs={{0,1},{1,2},{2,3},{3,4},{4,5},{5,6},{6,7},{8,9},{9,10},{10,11},{11... | collective-permute-start | bytes 98312 | tf_op jit(solution)/shard_map/ppermute | solution.py:24
  430.9 9.1 %collective-permute-start.48 = (bf16[128,128]{1,0:T(8,128)(2,1)S(1)}, bf16[128,128]{1,0:T(8,128)(2,1)S(1)}, u32[]{:S(2)}, u32[]{:S(2)}) collective-permute-start(bf16[128,128]{1,0:T(8,128)(2,1)S(1)} %get-tuple-element.68), channel_id=1, source_target_pairs={{0,8},{8,16},{16,24},{24,32},{32,40},{40,48},{48,56},{56,64},{64,7... | collective-permute-start | bytes 98312 | tf_op jit(solution)/shard_map/ppermute | solution.py:24
  460.6 7.0 %collective-permute-start.53 = (f32[6,128]{1,0:T(8,128)S(1)}, f32[6,128]{1,0:T(8,128)S(1)}, u32[]{:S(2)}, u32[]{:S(2)}) collective-permute-start(f32[6,128]{1,0:T(8,128)S(1)} %add.247), channel_id=1, source_target_pairs={{0,16},{8,24},{16,0},{24,8},{32,48},{40,56},{48,32},{56,40},{64,80... | collective-permute-start | bytes 9224 | tf_op jit(solution)/shard_map/ppermute | solution.py:42
  479.5 9.4 %collective-permute-start.56 = (f32[6,128]{1,0:T(8,128)S(1)}, f32[6,128]{1,0:T(8,128)S(1)}, u32[]{:S(2)}, u32[]{:S(2)}) collective-permute-start(f32[6,128]{1,0:T(8,128)S(1)} %add.250), channel_id=1, source_target_pairs={{0,128},{8,136},{16,144},{24,152},{32,160},{40,168},{48,176},{56,1... | collective-permute-start | bytes 9224 | tf_op jit(solution)/shard_map/ppermute | solution.py:42
  488.9 14.2 %collective-permute-start.57 = (f32[6,128]{1,0:T(8,128)S(1)}, f32[6,128]{1,0:T(8,128)S(1)}, u32[]{:S(2)}, u32[]{:S(2)}) collective-permute-start(f32[6,128]{1,0:T(8,128)S(1)} %add.251), channel_id=1, source_target_pairs={{0,256},{8,264},{16,272},{24,280},{32,288},{40,296},{48,304},{56,3... | collective-permute-start | bytes 9224 | tf_op jit(solution)/shard_map/ppermute | solution.py:42
  (25 other events, 422.6 us)
